TPU v7x, 512 devices: a whole 4x4x16 slice. The times are simulated.
512 devices in a mesh: dp: 64 (over z, x_lo, core), slab: 8 (over y, x_hi).
Axes of the slice: x: 4 (x_hi: 2, x_lo: 2; x = x_hi * 2 + x_lo), y: 4, z: 16, core: 2. Of those that a mesh axis runs over, the one named last changes fastest.
Arguments:
- voxels: bfloat16 [64, 8, 12, 32, 128], P('dp', None, None, 'slab'), may hold values from -16 to 16
- occupancy: int32 [64, 8, 12, 32], P('dp', None, None, 'slab'), may hold values 0 or 1
- out_grad: bfloat16 [64, 8, 12, 32, 128], P('dp', None, None, 'slab'), may hold values from -192 to 192
- weights: bfloat16 [2, 3456, 128], replicated, may hold values from -5 to 5
- master: float32 [2, 3456, 128], P(None, 'dp', 'slab'), may hold values from -5 to 5
- moment: float32 [2, 3456, 128], P(None, 'dp', 'slab'), may hold values from -18 to 18
- second: float32 [2, 3456, 128], P(None, 'dp', 'slab'), may hold values from 1 to 10
- teacher: float32 [2, 3456, 128], P(None, 'dp', 'slab'), may hold values from -5 to 5
Outputs:
- new_master: float32 [2, 3456, 128], P(None, 'dp', 'slab')
- new_moment: float32 [2, 3456, 128], P(None, 'dp', 'slab')
- new_second: float32 [2, 3456, 128], P(None, 'dp', 'slab')
- new_teacher: float32 [2, 3456, 128], P(None, 'dp', 'slab')
- new_weights: bfloat16 [2, 3456, 128], P(None, None, 'slab')
All inputs are finite; a program needn't handle non-finite values. No bound on the sum of `occupancy` on one device may be relied on, other than what follows from the above.
Results may differ from a plain program's by a relative error of at most 0.0013.
Values may be sent and summed in bfloat16 or wider, within the bound.
No kernel may reach another device: no remote copies, remote signals or barrier semaphores. Data moves between devices by JAX's collectives and lax.ppermute only.
A program may use at most 64 MiB of HBM per device.

v0:
```python
import jax
import jax.numpy as jnp
from jax import lax
from jax.sharding import PartitionSpec as P

C = 128
TAPS = 27
STEP_COUNT = 10
beta_first = 0.9
beta_second = 0.999
learning_rate = 0.01
weight_decay = 0.05
teacher_keep = 0.99
adam_epsilon = 1e-08


def with_halo(cells, sides, width):
    for axis, dim in sides:
        count = lax.axis_size(axis)
        ends = count - 1
        head = lax.slice_in_dim(cells, 0, width, axis=dim)
        tail = lax.slice_in_dim(cells, cells.shape[dim] - width, cells.shape[dim], axis=dim)
        cells = jnp.concatenate(
            [
                lax.ppermute(tail, axis, [(i, (i + 1) % count) for i in range(ends)]),
                cells,
                lax.ppermute(head, axis, [((i + 1) % count, i) for i in range(ends)]),
            ],
            axis=dim,
        )
    return cells


def tap_corners():
    return [
        (along_x, along_y, along_z)
        for along_x in range(3)
        for along_y in range(3)
        for along_z in range(3)
    ]


def unit_scale():
    return (TAPS * C) ** (-0.5)


def silu_slope(values):
    logistic = jax.nn.sigmoid(values)
    return logistic * (1.0 + values * (1.0 - logistic))


def take_window(padded, start, extent):
    window = padded[
        start[0] : start[0] + extent[0],
        start[1] : start[1] + extent[1],
        start[2] : start[2] + extent[2],
    ]
    return window.reshape(-1, window.shape[-1])


def forward_conv(padded, weight_rows, extent):
    channels = weight_rows.shape[1]
    summed = jnp.zeros((extent[0] * extent[1] * extent[2], channels), jnp.float32)
    for tap_index, corner in enumerate(tap_corners()):
        window = take_window(padded, corner, extent)
        block = weight_rows[tap_index * channels : (tap_index + 1) * channels]
        summed = summed + jnp.dot(window, block, preferred_element_type=jnp.float32)
    return (summed * unit_scale()).reshape(extent + (channels,))


def transposed_conv(padded_grad, weight_rows, extent):
    channels = weight_rows.shape[1]
    summed = jnp.zeros((extent[0] * extent[1] * extent[2], channels), jnp.float32)
    for tap_index, corner in enumerate(tap_corners()):
        start = (2 - corner[0], 2 - corner[1], 2 - corner[2])
        window = take_window(padded_grad, start, extent)
        block = weight_rows[tap_index * channels : (tap_index + 1) * channels]
        summed = summed + lax.dot_general(
            window, block, (((1,), (1,)), ((), ())), preferred_element_type=jnp.float32
        )
    return (summed * unit_scale()).reshape(extent + (channels,))


def weight_grad(padded, grad_field, extent):
    grad_rows = grad_field.reshape(-1, grad_field.shape[-1])
    blocks = []
    for corner in tap_corners():
        window = take_window(padded, corner, extent)
        blocks.append(
            lax.dot_general(
                window, grad_rows, (((0,), (0,)), ((), ())), preferred_element_type=jnp.float32
            )
        )
    return jnp.concatenate(blocks, axis=0) * unit_scale()


def adam_update(master, moment, second, teacher, gradient):
    new_moment = beta_first * moment + (1.0 - beta_first) * gradient
    new_second = beta_second * second + (1.0 - beta_second) * gradient * gradient
    first_fix = 1.0 - beta_first**STEP_COUNT
    second_fix = 1.0 - beta_second**STEP_COUNT
    ratio = new_moment / first_fix / (jnp.sqrt(new_second / second_fix) + adam_epsilon)
    new_master = master - learning_rate * (ratio + weight_decay * master)
    new_teacher = teacher_keep * teacher + (1.0 - teacher_keep) * new_master
    return (new_master, new_moment, new_second, new_teacher)


def local(voxels, occupancy, out_grad, weights, master, moment, second, teacher):
    own_cells = voxels[0]
    extent = tuple(own_cells.shape[:3])
    occupied = occupancy[0].astype(jnp.float32)[..., None]
    plane_pad = ((1, 1), (1, 1), (0, 0), (0, 0))
    rim_input = with_halo(own_cells, (("slab", 2),), 1)
    padded_in = jnp.pad(rim_input, plane_pad)
    pre_one = forward_conv(padded_in, weights[0], extent)
    act_one = (occupied * jax.nn.silu(pre_one)).astype(jnp.bfloat16)
    rim_hidden = with_halo(act_one, (("slab", 2),), 1)
    padded_act = jnp.pad(rim_hidden, plane_pad)
    pre_two = forward_conv(padded_act, weights[1], extent)
    grad_two = (out_grad[0].astype(jnp.float32) * occupied * silu_slope(pre_two)).astype(
        jnp.bfloat16
    )
    rim_grad = with_halo(grad_two, (("slab", 2),), 1)
    padded_grad = jnp.pad(rim_grad, plane_pad)
    wgrad_two = weight_grad(padded_act, grad_two, extent)
    back_one = transposed_conv(padded_grad, weights[1], extent)
    grad_one = (back_one * occupied * silu_slope(pre_one)).astype(jnp.bfloat16)
    wgrad_one = weight_grad(padded_in, grad_one, extent)
    weight_grads = jnp.stack([wgrad_one, wgrad_two])
    row_sums = lax.psum_scatter(weight_grads, "dp", scatter_dimension=1, tiled=True)
    gradient = lax.psum_scatter(row_sums, "slab", scatter_dimension=2, tiled=True)
    new_master, new_moment, new_second, new_teacher = adam_update(
        master, moment, second, teacher, gradient
    )
    fresh_weights = new_master.astype(jnp.bfloat16)
    new_weights = lax.all_gather(fresh_weights, "dp", axis=1, tiled=True)
    return (new_master, new_moment, new_second, new_teacher, new_weights)


def solution(mesh):
    in_specs = (
        P("dp", None, None, "slab", None),
        P("dp", None, None, "slab"),
        P("dp", None, None, "slab", None),
        P(),
        P(None, "dp", "slab"),
        P(None, "dp", "slab"),
        P(None, "dp", "slab"),
        P(None, "dp", "slab"),
    )
    out_specs = (
        P(None, "dp", "slab"),
        P(None, "dp", "slab"),
        P(None, "dp", "slab"),
        P(None, "dp", "slab"),
        P(None, None, "slab"),
    )
    return jax.shard_map(local, mesh=mesh, in_specs=in_specs, out_specs=out_specs, check_vma=False)
```

profile of v0, /device:TPU:1, one launch (start us, length us, event | category | flops | bytes accessed | tf_op | source)
XLA Modules:
  0.0 662.1 jit_solution(6944818351448994479)
XLA Ops:
  7.2 0.9 copy.675
  8.1 5.5 collective-permute-start
  13.6 1.3 collective-permute-start.1
  14.9 0.9 copy_convert_fusion
  15.9 0.7 fusion.352
  16.9 2.9 collective-permute-done.1
  20.0 0.6 fusion.347
  21.9 0.8 copy-done
  27.4 4.0 collective-permute-start.2
  31.4 1.3 collective-permute-start.3
  32.8 4.7 collective-permute-done.3
  37.7 0.3 fusion.345
  44.3 4.6 collective-permute-start.4
  48.9 1.5 collective-permute-start.5
  53.2 0.3 fusion.18
  56.9 0.3 fusion.343
  60.9 0.2 convolution_add_fusion.13
  64.2 0.2 fusion.53
  64.4 0.2 fusion.52
  64.6 0.2 fusion.51
  64.9 0.2 fusion.50
  65.1 0.2 fusion.49
  65.4 0.2 fusion.48
  65.6 0.2 fusion.47
  66.1 0.2 fusion.45
  66.3 0.2 fusion.44
  66.5 0.2 fusion.5
  67.0 0.2 fusion.4
  67.3 0.2 fusion.42
  67.5 0.2 fusion.41
  67.7 0.2 fusion.40
  68.7 0.2 fusion.36
  68.9 0.2 fusion.35
  69.2 0.2 fusion.34
  69.4 0.2 fusion.33
  69.6 0.2 fusion.32
  69.9 0.2 fusion.31
  70.3 0.2 pad_maximum_fusion
  70.5 14.0 %copy.534 = f32[2,3456,128]{2,0,1:T(2,128)} copy(f32[2,3456,128]{2,1,0:T(8,128)S(1)} %pad_maximum_fusion) | data formatting | bytes 7077888 | tf_op jit(solution)/shard_map/stack | solution.py:129
  84.5 1.3 dynamic-slice
  85.8 1.3 dynamic-slice.2
  88.4 449.9 %all-reduce.7.cloned.1.call-done = f32[2,3456,128]{2,0,1:T(2,128)} async-done(((f32[2,3456,128]{2,0,1:T(2,128)}), f32[2,3456,128]{2,0,1:T(2,128)}) %all-reduce.7.cloned.1.call-update) | async-done | bytes 3538960
  538.3 0.8 constant_dynamic-slice_fusion.1
  539.2 36.3 %all-reduce.4 = f32[2,54,128]{1,0,2:T(2,128)S(1)} all-reduce(f32[2,54,128]{1,0,2:T(2,128)S(1)} %copy.535), channel_id=3, replica_groups=mesh['dp'=64,'slab'=8] {'slab'}, use_global_device_ids=true, to_apply=%region_1.2.clone | all-reduce | flops 13824 | bytes 110592
  575.6 0.6 fusion.341
  576.4 75.2 %all_gather.3 = bf16[2,3456,16]{2,0,1:T(2,128)(2,1)S(1)} all-gather(bf16[2,54,16]{2,0,1:T(2,128)(2,1)S(1)} %copy.539), channel_id=1, replica_groups=mesh['dp'=64,'slab'=8] {'dp'}, dimensions={1}, use_global_device_ids=true | all-gather | bytes 224640 | tf_op jit(solution)/shard_map/all_gather | solution.py:136
  651.6 3.0 copy.540
  654.6 0.6 multiply_add_fusion
  (237 shorter events, 26.4 us)
Async XLA Ops:
  7.2 531.1 %all-reduce.7.cloned.1.call-start = ((), (), s32[]{:S(2)}) async-start(), calls=%async_computation | async-start | bytes 7077888
  8.1 8.8 %collective-permute-start = (bf16[8,12,1,128]{3,1,2,0:T(8,128)(2,1)S(1)}, bf16[8,12,1,128]{3,1,2,0:T(8,128)(2,1)S(1)}, u32[]{:S(2)}, u32[]{:S(2)}) collective-permute-start(bf16[8,12,1,128]{3,1,2,0:T(8,128)(2,1)S(1)} %get-tuple-element.110), channel_id=1, source_target_pairs={{0,1},{1,2},{2,3},{3,4},{4,5},{5,6},{6,7},{8,9},{9,10},{10,11},{11... | collective-permute-start | bytes 73736 | tf_op jit(solution)/shard_map/ppermute | solution.py:25
  13.6 6.2 collective-permute-start.1
  21.1 1.5 copy-start
  23.6 1.2 copy-start.1
  27.4 5.4 collective-permute-start.2
  31.4 6.1 collective-permute-start.3
  42.7 1.2 copy-start.2
  44.3 12.4 %collective-permute-start.4 = (bf16[8,12,1,128]{3,0,2,1:T(8,128)(2,1)S(1)}, bf16[8,12,1,128]{3,0,2,1:T(8,128)(2,1)S(1)}, u32[]{:S(2)}, u32[]{:S(2)}) collective-permute-start(bf16[8,12,1,128]{3,0,2,1:T(8,128)(2,1)S(1)} %get-tuple-element.114), channel_id=1, source_target_pairs={{0,1},{1,2},{2,3},{3,4},{4,5},{5,6},{6,7},{8,9},{9,10},{10,11},{11... | collective-permute-start | bytes 73736 | tf_op jit(solution)/shard_map/ppermute | solution.py:25
  48.9 7.7 %collective-permute-start.5 = (bf16[8,12,1,128]{3,0,2,1:T(8,128)(2,1)S(1)}, bf16[8,12,1,128]{3,0,2,1:T(8,128)(2,1)S(1)}, u32[]{:S(2)}, u32[]{:S(2)}) collective-permute-start(bf16[8,12,1,128]{3,0,2,1:T(8,128)(2,1)S(1)} %get-tuple-element.115), channel_id=1, source_target_pairs={{1,0},{2,1},{3,2},{4,3},{5,4},{6,5},{7,6},{9,8},{10,9},{11,10},{12... | collective-permute-start | bytes 73736 | tf_op jit(solution)/shard_map/ppermute | solution.py:27
  84.5 491.1 %copy-start.4 = (f32[2,54,16]{1,2,0:T(8,128)S(1)}, f32[2,54,16]{1,2,0:T(8,128)}, u32[]{:S(2)}) copy-start(f32[2,54,16]{1,2,0:T(8,128)} %param.12) | copy-start | bytes 20740
  84.5 491.1 %copy-start.5 = (f32[2,54,16]{1,2,0:T(8,128)S(1)}, f32[2,54,16]{1,2,0:T(8,128)}, u32[]{:S(2)}) copy-start(f32[2,54,16]{1,2,0:T(8,128)} %param.13) | copy-start | bytes 20740
  84.5 491.1 %copy-start.6 = (f32[2,54,16]{1,2,0:T(8,128)S(1)}, f32[2,54,16]{1,2,0:T(8,128)}, u32[]{:S(2)}) copy-start(f32[2,54,16]{1,2,0:T(8,128)} %param.14) | copy-start | bytes 20740
  576.2 78.3 %copy-start.3 = (f32[2,54,16]{1,2,0:T(8,128)}, f32[2,54,16]{1,2,0:T(8,128)S(1)}, u32[]{:S(2)}) copy-start(f32[2,54,16]{1,2,0:T(8,128)S(1)} %get-tuple-element.31) | copy-start | bytes 20740
  576.4 78.2 %copy-start.7 = (f32[2,54,16]{1,2,0:T(8,128)S(1)}, f32[2,54,16]{1,2,0:T(8,128)}, u32[]{:S(2)}) copy-start(f32[2,54,16]{1,2,0:T(8,128)} %param.15) | copy-start | bytes 20740
Sparse Core Ops, SparseCore 0:
  84.6 453.6 all-reduce.6
where the time goes:
time: 663 us; the launch traced here: 662 us
  waiting for transfers between devices  458 us (69%)
  blocking collectives  112 us (17%)
  local copies, waits for them, and re-layouts  27.2 us (4%)
  matrix products  26.2 us (4%)
  starting transfers between devices  18.3 us (3%)
  between operations  16.9 us (3%)
    unnamed x2, waiting for transfers between devices  450 us
    all_gather x1, blocking collectives, local(): new_weights = lax.all_gather(fresh_weights, 'dp', axis=1, tiled=True)  75.2 us
    unnamed x1, blocking collectives  36.3 us
    ppermute x3, starting transfers between devices, with_halo(): lax.ppermute(tail, axis, [(i, (i + 1) % count) for i in range(ends)])  14.2 us
    another operation x1, local copies, waits for them, and re-layouts, local(): weight_grads = jnp.stack([wgrad_one, wgrad_two])  14 us
  transfers between devices with their start and end apart: 7, of which 3 were waited for; matrix products, arithmetic and copies ran while one was open for 2% of the time, Pallas kernels for 0%

commit v1 on v0

--- a/solution.py
+++ b/solution.py
@@ -133,7 +133,9 @@
         master, moment, second, teacher, gradient
     )
     fresh_weights = new_master.astype(jnp.bfloat16)
-    new_weights = lax.all_gather(fresh_weights, "dp", axis=1, tiled=True)
+    new_weights = jnp.concatenate(
+        lax.all_to_all(jnp.stack([fresh_weights] * lax.axis_size("dp")), "dp", 0, 0), axis=1
+    )
     return (new_master, new_moment, new_second, new_teacher, new_weights)
 
 

time: 663 us -> 630 us (0.950)
  blocking collectives: 112 us -> 36.3 us
  starting transfers between devices: 18.3 us -> 39.1 us
  waiting for transfers between devices: 458 us -> 478 us
    all_gather x1 -> x0, blocking collectives: 75.2 us -> none  [local(): new_weights = lax.all_gather(fresh_weights, 'dp', axis=1, tiled=True)]
    all_to_all x0 -> x1, starting transfers between devices: none -> 20.9 us  [local(): lax.all_to_all(jnp.stack([fresh_weights] * lax.axis_size('dp')), 'dp', 0, 0)]
    all_to_all x0 -> x1, waiting for transfers between devices: none -> 20.3 us  [local(): lax.all_to_all(jnp.stack([fresh_weights] * lax.axis_size('dp')), 'dp', 0, 0)]
  transfers between devices with their start and end apart: 7 -> 8, of which waited for: 3 -> 4; matrix products, arithmetic and copies ran while one was open for 2% -> 2% of each run, Pallas kernels for 0% -> 0%
where the time goes in v1:
time: 630 us; the launch traced here: 629 us
  waiting for transfers between devices  478 us (76%)
  starting transfers between devices  39.1 us (6%)
  blocking collectives  36.3 us (6%)
  local copies, waits for them, and re-layouts  28.1 us (4%)
  matrix products  26.2 us (4%)
  between operations  17 us (3%)
    unnamed x2, waiting for transfers between devices  450 us
    unnamed x1, blocking collectives  36.3 us
    all_to_all x1, starting transfers between devices, local(): lax.all_to_all(jnp.stack([fresh_weights] * lax.axis_size('dp')), 'dp', 0, 0)  20.9 us
    all_to_all x1, waiting for transfers between devices, local(): lax.all_to_all(jnp.stack([fresh_weights] * lax.axis_size('dp')), 'dp', 0, 0)  20.3 us
    ppermute x3, starting transfers between devices, with_halo(): lax.ppermute(tail, axis, [(i, (i + 1) % count) for i in range(ends)])  14.2 us
    another operation x1, local copies, waits for them, and re-layouts, local(): weight_grads = jnp.stack([wgrad_one, wgrad_two])  13.9 us
  transfers between devices with their start and end apart: 8, of which 4 were waited for; matrix products, arithmetic and copies ran while one was open for 2% of the time, Pallas kernels for 0%

profile of v1, /device:TPU:1, one launch (start us, length us, event | category | flops | bytes accessed | tf_op | source)
XLA Modules:
  0.0 629.0 jit_solution(5979622858788280141)
XLA Ops:
  7.2 0.9 copy.673
  8.1 5.5 collective-permute-start
  13.6 1.3 collective-permute-start.1
  14.9 0.9 copy_convert_fusion
  15.9 0.7 fusion.352
  16.9 2.9 collective-permute-done.1
  20.0 0.4 fusion.347
  21.7 0.8 copy-done
  27.2 4.0 collective-permute-start.2
  31.3 1.3 collective-permute-start.3
  32.7 4.7 collective-permute-done.3
  37.5 0.3 fusion.345
  44.1 4.6 collective-permute-start.4
  48.8 1.5 collective-permute-start.5
  53.0 0.3 fusion.18
  56.8 0.3 fusion.343
  60.7 0.2 convolution_add_fusion.13
  64.3 0.2 fusion.52
  64.5 0.2 fusion.51
  64.8 0.2 fusion.50
  65.0 0.2 fusion.49
  65.2 0.2 fusion.48
  65.5 0.2 fusion.47
  66.4 0.2 fusion.5
  66.9 0.2 fusion.4
  67.1 0.2 fusion.42
  67.4 0.2 fusion.41
  67.6 0.2 fusion.40
  68.6 0.2 fusion.36
  68.8 0.2 fusion.35
  69.1 0.2 fusion.34
  69.3 0.2 fusion.33
  69.5 0.2 fusion.32
  69.8 0.2 fusion.31
  70.2 0.2 pad_maximum_fusion
  70.4 13.9 %copy.533 = f32[2,3456,128]{2,0,1:T(2,128)} copy(f32[2,3456,128]{2,1,0:T(8,128)S(1)} %pad_maximum_fusion) | data formatting | bytes 7077888 | tf_op jit(solution)/shard_map/stack | solution.py:129
  84.4 1.3 dynamic-slice
  85.7 1.3 dynamic-slice.2
  88.3 449.9 %all-reduce.7.cloned.1.call-done = f32[2,3456,128]{2,0,1:T(2,128)} async-done(((f32[2,3456,128]{2,0,1:T(2,128)}), f32[2,3456,128]{2,0,1:T(2,128)}) %all-reduce.7.cloned.1.call-update) | async-done | bytes 3538960
  538.1 0.8 constant_dynamic-slice_fusion.1
  539.1 36.3 %all-reduce.4 = f32[2,54,128]{1,0,2:T(2,128)S(1)} all-reduce(f32[2,54,128]{1,0,2:T(2,128)S(1)} %copy.534), channel_id=3, replica_groups=mesh['dp'=64,'slab'=8] {'slab'}, use_global_device_ids=true, to_apply=%region_1.2.clone | all-reduce | flops 13824 | bytes 110592
  575.5 0.6 fusion.341
  576.2 1.6 reshape.1275
  577.8 20.9 %all-to-all-start = ((bf16[64,2,864]{2,1,0:T(2,128)(2,1)}), bf16[64,2,864]{2,1,0:T(2,128)(2,1)S(1)}, u32[]{:S(2)}, u32[]{:S(2)}) async-start(bf16[64,2,864]{2,1,0:T(2,128)(2,1)} %reshape.1275), calls=%async_computation | async-start | bytes 458752 | tf_op jit(solution)/shard_map/all_to_all | solution.py:137
  598.7 0.6 multiply_add_fusion
  599.3 20.3 %all-to-all-done = bf16[64,2,864]{2,1,0:T(2,128)(2,1)S(1)} async-done(((bf16[64,2,864]{2,1,0:T(2,128)(2,1)}), bf16[64,2,864]{2,1,0:T(2,128)(2,1)S(1)}, u32[]{:S(2)}, u32[]{:S(2)}) %all-to-all-start) | async-done | bytes 221216 | tf_op jit(solution)/shard_map/all_to_all | solution.py:137
  619.6 0.9 reshape.1276
  620.8 1.4 reshape.1216
  (242 shorter events, 27.3 us)
Async XLA Ops:
  7.2 531.0 %all-reduce.7.cloned.1.call-start = ((), (), s32[]{:S(2)}) async-start(), calls=%async_computation.1 | async-start | bytes 7077888
  8.1 8.8 %collective-permute-start = (bf16[8,12,1,128]{3,1,2,0:T(8,128)(2,1)S(1)}, bf16[8,12,1,128]{3,1,2,0:T(8,128)(2,1)S(1)}, u32[]{:S(2)}, u32[]{:S(2)}) collective-permute-start(bf16[8,12,1,128]{3,1,2,0:T(8,128)(2,1)S(1)} %get-tuple-element.100), channel_id=1, source_target_pairs={{0,1},{1,2},{2,3},{3,4},{4,5},{5,6},{6,7},{8,9},{9,10},{10,11},{11... | collective-permute-start | bytes 73736 | tf_op jit(solution)/shard_map/ppermute | solution.py:25
  13.6 6.2 collective-permute-start.1
  21.0 1.5 copy-start
  23.5 1.2 copy-start.1
  27.2 5.4 collective-permute-start.2
  31.3 6.1 collective-permute-start.3
  42.5 1.2 copy-start.2
  44.1 12.4 %collective-permute-start.4 = (bf16[8,12,1,128]{3,0,2,1:T(8,128)(2,1)S(1)}, bf16[8,12,1,128]{3,0,2,1:T(8,128)(2,1)S(1)}, u32[]{:S(2)}, u32[]{:S(2)}) collective-permute-start(bf16[8,12,1,128]{3,0,2,1:T(8,128)(2,1)S(1)} %get-tuple-element.104), channel_id=1, source_target_pairs={{0,1},{1,2},{2,3},{3,4},{4,5},{5,6},{6,7},{8,9},{9,10},{10,11},{11... | collective-permute-start | bytes 73736 | tf_op jit(solution)/shard_map/ppermute | solution.py:25
  48.8 7.7 %collective-permute-start.5 = (bf16[8,12,1,128]{3,0,2,1:T(8,128)(2,1)S(1)}, bf16[8,12,1,128]{3,0,2,1:T(8,128)(2,1)S(1)}, u32[]{:S(2)}, u32[]{:S(2)}) collective-permute-start(bf16[8,12,1,128]{3,0,2,1:T(8,128)(2,1)S(1)} %get-tuple-element.105), channel_id=1, source_target_pairs={{1,0},{2,1},{3,2},{4,3},{5,4},{6,5},{7,6},{9,8},{10,9},{11,10},{12... | collective-permute-start | bytes 73736 | tf_op jit(solution)/shard_map/ppermute | solution.py:27
  84.4 491.1 %copy-start.4 = (f32[2,54,16]{1,2,0:T(8,128)S(1)}, f32[2,54,16]{1,2,0:T(8,128)}, u32[]{:S(2)}) copy-start(f32[2,54,16]{1,2,0:T(8,128)} %param.12) | copy-start | bytes 20740
  84.4 491.1 %copy-start.5 = (f32[2,54,16]{1,2,0:T(8,128)S(1)}, f32[2,54,16]{1,2,0:T(8,128)}, u32[]{:S(2)}) copy-start(f32[2,54,16]{1,2,0:T(8,128)} %param.13) | copy-start | bytes 20740
  84.4 491.1 %copy-start.6 = (f32[2,54,16]{1,2,0:T(8,128)S(1)}, f32[2,54,16]{1,2,0:T(8,128)}, u32[]{:S(2)}) copy-start(f32[2,54,16]{1,2,0:T(8,128)} %param.14) | copy-start | bytes 20740
  84.4 514.3 %copy-start.7 = (f32[2,54,16]{1,2,0:T(8,128)S(1)}, f32[2,54,16]{1,2,0:T(8,128)}, u32[]{:S(2)}) copy-start(f32[2,54,16]{1,2,0:T(8,128)} %param.15) | copy-start | bytes 20740
  576.1 44.4 %copy-start.3 = (f32[2,54,16]{1,2,0:T(8,128)}, f32[2,54,16]{1,2,0:T(8,128)S(1)}, u32[]{:S(2)}) copy-start(f32[2,54,16]{1,2,0:T(8,128)S(1)} %get-tuple-element.21) | copy-start | bytes 20740
  577.8 41.8 %all-to-all-start = ((bf16[64,2,864]{2,1,0:T(2,128)(2,1)}), bf16[64,2,864]{2,1,0:T(2,128)(2,1)S(1)}, u32[]{:S(2)}, u32[]{:S(2)}) async-start(bf16[64,2,864]{2,1,0:T(2,128)(2,1)} %reshape.1275), calls=%async_computation | async-start | bytes 458752 | tf_op jit(solution)/shard_map/all_to_all | solution.py:137
Sparse Core Ops, SparseCore 0:
  84.5 453.5 all-reduce.6
